TPU v7x, 256 devices: a whole 4x4x8 slice. The times are simulated.
256 devices in a mesh: dp: 4 (over y_lo, core), row: 8 (over y_hi, x), col: 8 (over z).
Axes of the slice: x: 4, y: 4 (y_hi: 2, y_lo: 2; y = y_hi * 2 + y_lo), z: 8, core: 2. Of those that a mesh axis runs over, the one named last changes fastest.
Arguments:
- tokens: bfloat16 [3072, 4096], P('dp', ('row', 'col')), may hold values from -6 to 6
- cotangent: bfloat16 [3072, 4096], P('dp', ('row', 'col')), may hold values from -4 to 4
- gate_weight: bfloat16 [4096, 14336], P('row', 'col'), may hold values from -0.09375 to 0.09375
- up_weight: bfloat16 [4096, 14336], P('row', 'col'), may hold values from -0.09375 to 0.09375
- down_weight: bfloat16 [14336, 4096], P('col', 'row'), may hold values from -0.046875 to 0.046875
Outputs:
- layer_out: bfloat16 [3072, 4096], P(('dp', 'col'), 'row')
- input_grad: bfloat16 [3072, 4096], P(('dp', 'col'), 'row')
- gate_wgrad: bfloat16 [4096, 14336], P('row', 'col')
- up_wgrad: bfloat16 [4096, 14336], P('row', 'col')
- down_wgrad: bfloat16 [14336, 4096], P('col', 'row')
All inputs are finite; a program needn't handle non-finite values.
Results may differ from a plain program's by a relative error of at most 0.034.
Values may be sent and summed in bfloat16 or wider, within the bound.
No kernel may reach another device: no remote copies, remote signals or barrier semaphores. Data moves between devices by JAX's collectives and lax.ppermute only.
A program may use at most 128 MiB of HBM per device.

v0:
```python
import jax
import jax.numpy as jnp
from jax import lax
from jax.sharding import PartitionSpec as P


def contract_rows(left, right):
    return lax.dot_general(
        left, right, (((0,), (0,)), ((), ())), preferred_element_type=jnp.float32
    )


def contract_cols(left, right):
    return lax.dot_general(
        left, right, (((1,), (1,)), ((), ())), preferred_element_type=jnp.float32
    )


def local(tokens, cotangent, gate_weight, up_weight, down_weight):
    f32 = jnp.float32
    whole_x, whole_dy = (
        lax.all_gather(tokens, "col", axis=1, tiled=True),
        lax.all_gather(cotangent, "col", axis=1, tiled=True),
    )
    width = gate_weight.shape[1]
    rows = whole_x
    stacked = lax.psum_scatter(
        jnp.concatenate(
            [
                jnp.dot(rows, gate_weight, preferred_element_type=f32),
                jnp.dot(rows, up_weight, preferred_element_type=f32),
            ],
            axis=1,
        ).astype(jnp.bfloat16),
        "row",
        scatter_dimension=0,
        tiled=True,
    ).astype(jnp.float32)
    gate = stacked[:, :width]
    up = stacked[:, width:]
    sigma = jax.nn.sigmoid(gate)
    silu_gate = gate * sigma
    hidden = (silu_gate * up).astype(jnp.bfloat16)
    hidden_all = lax.all_gather(hidden, "row", axis=0, tiled=True)
    out_terms = jnp.dot(hidden_all, down_weight, preferred_element_type=f32)
    layer_out = lax.psum_scatter(
        out_terms.astype(jnp.bfloat16), "col", scatter_dimension=0, tiled=True
    )
    down_part = contract_rows(hidden_all, whole_dy).astype(jnp.bfloat16)
    rows = whole_dy
    hidden_grad = lax.psum_scatter(
        contract_cols(rows, down_weight).astype(jnp.bfloat16),
        "row",
        scatter_dimension=0,
        tiled=True,
    ).astype(jnp.float32)
    gate_grad = (hidden_grad * up * sigma * (1.0 + gate * (1.0 - sigma))).astype(jnp.bfloat16)
    up_grad = (hidden_grad * silu_gate).astype(jnp.bfloat16)
    gate_all, up_all = (
        lax.all_gather(gate_grad, "row", axis=0, tiled=True),
        lax.all_gather(up_grad, "row", axis=0, tiled=True),
    )
    input_grad = lax.psum_scatter(
        (contract_cols(gate_all, gate_weight) + contract_cols(up_all, up_weight)).astype(
            jnp.bfloat16
        ),
        "col",
        scatter_dimension=0,
        tiled=True,
    )
    gate_part = contract_rows(whole_x, gate_all).astype(jnp.bfloat16)
    up_part = contract_rows(whole_x, up_all).astype(jnp.bfloat16)
    gate_sum, up_sum, down_sum = (
        lax.psum(gate_part.astype(f32).astype(jnp.bfloat16), "dp").astype(jnp.float32),
        lax.psum(up_part.astype(f32).astype(jnp.bfloat16), "dp").astype(jnp.float32),
        lax.psum(down_part.astype(f32).astype(jnp.bfloat16), "dp").astype(jnp.float32),
    )
    gate_wgrad = gate_sum.astype(jnp.bfloat16)
    up_wgrad = up_sum.astype(jnp.bfloat16)
    down_wgrad = down_sum.astype(jnp.bfloat16)
    return (layer_out, input_grad, gate_wgrad, up_wgrad, down_wgrad)


def solution(mesh):
    in_specs = (
        P("dp", ("row", "col")),
        P("dp", ("row", "col")),
        P("row", "col"),
        P("row", "col"),
        P("col", "row"),
    )
    out_specs = (
        P(("dp", "col"), "row"),
        P(("dp", "col"), "row"),
        P("row", "col"),
        P("row", "col"),
        P("col", "row"),
    )
    return jax.shard_map(local, mesh=mesh, in_specs=in_specs, out_specs=out_specs, check_vma=False)
```

profile of v0, /device:TPU:2, one launch (start us, length us, event | category | flops | bytes accessed | tf_op | source)
XLA Modules:
  0.0 643.3 jit_solution(17645886271046592666)
XLA Ops:
  7.2 0.0 copy-start
  7.2 0.0 reduce-scatter.5.cloned.1.call-start
  7.2 30.2 %all_gather.15 = bf16[768,512]{0,1:T(8,128)(2,1)S(1)} all-gather(bf16[768,64]{0,1:T(8,128)(2,1)} %param.5), channel_id=1, replica_groups=mesh['dp'=4,'row'=8,'col'=8] {'col'}, dimensions={1}, use_global_device_ids=true | all-gather | bytes 884736 | tf_op jit(solution)/shard_map/all_gather | solution.py:22
  37.4 3.5 convolution_convert_fusion.1
  40.9 1.6 convolution_convert_fusion.2
  42.5 2.8 pad_maximum_fusion
  45.4 0.0 reduce-scatter.5.cloned.1.call-update
  45.4 0.0 reduce-scatter.9.cloned.1.call-start
  45.4 0.8 copy-done.4
  46.2 26.1 %all_gather.17 = bf16[768,512]{0,1:T(8,128)(2,1)S(1)} all-gather(bf16[768,64]{0,1:T(8,128)(2,1)S(1)} %copy-done.4), channel_id=1, replica_groups=mesh['dp'=4,'row'=8,'col'=8] {'col'}, dimensions={1}, use_global_device_ids=true | all-gather | bytes 884736 | tf_op jit(solution)/shard_map/all_gather | solution.py:23
  72.4 0.9 copy-done.3
  73.2 3.2 convolution_convert_fusion
  76.4 0.0 reduce-scatter.9.cloned.1.call-update
  76.4 0.0 all-gather.4.cloned.1.call-start
  76.5 66.3 %reduce-scatter.5.cloned.1.call-done = bf16[96,3584]{1,0:T(8,128)(2,1)} async-done(((bf16[768,3584]{1,0:T(8,128)(2,1)}), bf16[96,3584]{1,0:T(8,128)(2,1)}) %reduce-scatter.5.cloned.1.call-update) | async-done | bytes 688144 | tf_op jit(solution)/shard_map/reduce_scatter | solution.py:27
  142.8 1.2 convert_element_type.52
  144.0 86.2 %reduce-scatter.9.cloned.1.call-done = bf16[96,1792]{1,0:T(8,128)(2,1)} async-done(((bf16[768,1792]{1,0:T(8,128)(2,1)}), bf16[96,1792]{1,0:T(8,128)(2,1)}) %reduce-scatter.9.cloned.1.call-update) | async-done | bytes 344080 | tf_op jit(solution)/shard_map/reduce_scatter | solution.py:51
  230.1 2.3 fusion.5
  232.4 0.0 all-gather.4.cloned.1.call-update
  232.4 0.0 all-gather.6.cloned.1.call-start
  232.5 0.5 all-gather.6.cloned.1.call-update
  233.0 0.0 all-gather.8.cloned.1.call-start
  233.1 0.5 all-gather.8.cloned.1.call-update
  233.6 0.0 copy-start.2
  233.6 0.0 all-reduce.3.cloned.1.call-start
  233.7 63.4 %all-gather.4.cloned.1.call-done = bf16[768,1792]{1,0:T(8,128)(2,1)} async-done(((bf16[96,1792]{1,0:T(8,128)(2,1)}), bf16[768,1792]{1,0:T(8,128)(2,1)}) %all-gather.4.cloned.1.call-update) | async-done | bytes 2752528 | tf_op jit(solution)/shard_map/all_gather | solution.py:44
  297.0 4.8 convolution_convert_fusion.3
  301.9 61.3 %all-gather.6.cloned.1.call-done = bf16[768,1792]{1,0:T(8,128)(2,1)} async-done(((bf16[96,1792]{1,0:T(8,128)(2,1)}), bf16[768,1792]{1,0:T(8,128)(2,1)}) %all-gather.6.cloned.1.call-update) | async-done | bytes 2752528 | tf_op jit(solution)/shard_map/all_gather | solution.py:60
  363.2 4.7 fusion
  367.9 61.5 %all-gather.8.cloned.1.call-done = bf16[768,1792]{1,0:T(8,128)(2,1)} async-done(((bf16[96,1792]{1,0:T(8,128)(2,1)}), bf16[768,1792]{1,0:T(8,128)(2,1)}) %all-gather.8.cloned.1.call-update) | async-done | bytes 2752528 | tf_op jit(solution)/shard_map/all_gather | solution.py:61
  429.4 4.7 fusion.1
  434.1 0.0 all-reduce.3.cloned.1.call-update
  434.1 0.2 reduce-scatter.7.cloned.1.call-start
  434.3 4.2 convolution_convert_fusion.6
  438.5 0.0 reduce-scatter.7.cloned.1.call-update
  438.6 0.0 reduce-scatter.11.cloned.1.call-start
  438.6 0.0 copy-start.7
  438.6 4.1 fusion.7
  442.7 0.0 copy-done.5
  442.7 0.0 copy-done.7
  442.7 2.5 add_convert_fusion
  445.2 0.0 reduce-scatter.11.cloned.1.call-update
  445.3 105.7 %all-reduce.3.cloned.1.call-done = (bf16[512,1792]{0,1:T(8,128)(2,1)}, bf16[512,1792]{0,1:T(8,128)(2,1)}, bf16[1792,512]{1,0:T(8,128)(2,1)}) async-done(((bf16[512,1792]{0,1:T(8,128)(2,1)}, bf16[512,1792]{0,1:T(8,128)(2,1)}, bf16[1792,512]{1,0:T(8,128)(2,1)}), (bf16[512,1792]{0,1:T(8,128)(2,1)}, bf16[512,1792]{0,1:T(8,128)(2,1)}, bf16[1792,512]{1,0:T(8,128)(2,1)})) %all-reduce.3.cloned.1.call-update) | async-done | bytes 5505040 | tf_op jit(solution)/shard_map/psum | solution.py:74
  551.0 3.8 copy.10
  554.8 3.8 copy.11
  558.5 35.0 %reduce-scatter.7.cloned.1.call-done = bf16[96,512]{1,0:T(8,128)(2,1)} async-done(((bf16[768,512]{1,0:T(8,128)(2,1)}), bf16[96,512]{1,0:T(8,128)(2,1)}) %reduce-scatter.7.cloned.1.call-update) | async-done | bytes 98320 | tf_op jit(solution)/shard_map/reduce_scatter | solution.py:46
  593.5 40.1 %reduce-scatter.11.cloned.1.call-done = bf16[96,512]{1,0:T(8,128)(2,1)} async-done(((bf16[768,512]{1,0:T(8,128)(2,1)}), bf16[96,512]{1,0:T(8,128)(2,1)}) %reduce-scatter.11.cloned.1.call-update) | async-done | bytes 98320 | tf_op jit(solution)/shard_map/reduce_scatter | solution.py:63
  633.6 2.8 copy.15
  (9 shorter events, 0.0 us)
Async XLA Ops:
  7.2 66.1 %copy-start = (bf16[1792,512]{1,0:T(8,128)(2,1)S(1)}, bf16[1792,512]{1,0:T(8,128)(2,1)}, u32[]{:S(2)}) copy-start(bf16[1792,512]{1,0:T(8,128)(2,1)} %param.9) | copy-start | bytes 5505028
  7.2 135.6 %reduce-scatter.5.cloned.1.call-start = ((), (), s32[]{:S(2)}) async-start(), calls=%async_computation.4 | async-start | bytes 6193152 | tf_op jit(solution)/shard_map/reduce_scatter | solution.py:27
  37.4 3.5 copy-start.1
  37.4 3.5 copy-start.6
  45.3 0.9 copy-start.4
  45.4 184.8 %reduce-scatter.9.cloned.1.call-start = ((), (), s32[]{:S(2)}) async-start(), calls=%async_computation.7 | async-start | bytes 3096576 | tf_op jit(solution)/shard_map/reduce_scatter | solution.py:51
  72.4 0.9 copy-start.3
  76.4 220.6 %all-gather.4.cloned.1.call-start = ((), (), s32[]{:S(2)}) async-start(), calls=%async_computation.5 | async-start | bytes 3096576 | tf_op jit(solution)/shard_map/all_gather | solution.py:44
  232.4 130.8 %all-gather.6.cloned.1.call-start = ((), (), s32[]{:S(2)}) async-start(), calls=%async_computation.8 | async-start | bytes 3096576 | tf_op jit(solution)/shard_map/all_gather | solution.py:60
  233.0 196.4 %all-gather.8.cloned.1.call-start = ((), (), s32[]{:S(2)}) async-start(), calls=%async_computation.9 | async-start | bytes 3096576 | tf_op jit(solution)/shard_map/all_gather | solution.py:61
  233.6 129.6 %copy-start.2 = (bf16[768,512]{0,1:T(8,128)(2,1)S(1)}, bf16[768,512]{0,1:T(8,128)(2,1)}, u32[]{:S(2)}) copy-start(bf16[768,512]{0,1:T(8,128)(2,1)} %copy-done.1) | copy-start | bytes 2359300
  233.6 317.3 %all-reduce.3.cloned.1.call-start = ((), (), s32[]{:S(2)}) async-start(), calls=%async_computation.11 | async-start | bytes 11010048 | tf_op jit(solution)/shard_map/psum | solution.py:74
  434.1 159.4 %reduce-scatter.7.cloned.1.call-start = ((), (), s32[]{:S(2)}) async-start(), calls=%async_computation.6 | async-start | bytes 884736 | tf_op jit(solution)/shard_map/reduce_scatter | solution.py:46
  438.6 195.1 %reduce-scatter.11.cloned.1.call-start = ((), (), s32[]{:S(2)}) async-start(), calls=%async_computation.10 | async-start | bytes 884736 | tf_op jit(solution)/shard_map/reduce_scatter | solution.py:63
  438.6 4.1 copy-start.5
  438.6 4.1 copy-start.7
Sparse Core Ops, SparseCore 0:
  45.5 97.2 reduce-scatter.4
  146.9 83.1 reduce-scatter.8
  233.3 63.6 all-gather.3
  299.5 63.6 all-gather.5
  365.7 63.6 all-gather.7
  434.2 116.7 all-reduce.2
  554.1 39.4 reduce-scatter.6
  596.6 36.9 reduce-scatter.10
where the time goes:
time: 644 us; the launch traced here: 643 us
  waiting for transfers between devices  521 us (81%)
  blocking collectives  56.3 us (9%)
  matrix products  33.2 us (5%)
  between operations  14.2 us (2%)
  local copies, waits for them, and re-layouts  12.2 us (2%)
    psum x1, waiting for transfers between devices, local(): lax.psum(gate_part.astype(f32).astype(jnp.bfloat16), 'dp')  106 us
    reduce_scatter x1, waiting for transfers between devices, local(): lax.psum_scatter(contract_cols(rows, down_weight).astype(jnp.bfloat16), '...  86.2 us
    reduce_scatter x1, waiting for transfers between devices, local(): lax.psum_scatter(jnp.concatenate([jnp.dot(rows, gate_weight, preferred_el...  66.3 us
    all_gather x1, waiting for transfers between devices, local(): hidden_all = lax.all_gather(hidden, 'row', axis=0, tiled=True)  63.4 us
    all_gather x1, waiting for transfers between devices, local(): lax.all_gather(up_grad, 'row', axis=0, tiled=True)  61.5 us
    all_gather x1, waiting for transfers between devices, local(): lax.all_gather(gate_grad, 'row', axis=0, tiled=True)  61.3 us
    reduce_scatter x1, waiting for transfers between devices, local(): lax.psum_scatter((contract_cols(gate_all, gate_weight) + contract_cols(up...  40.1 us
    reduce_scatter x1, waiting for transfers between devices, local(): lax.psum_scatter(out_terms.astype(jnp.bfloat16), 'col', scatter_dimension...  35 us
  transfers between devices with their start and end apart: 8, of which 8 were waited for; matrix products, arithmetic and copies ran while one was open for 5% of the time, Pallas kernels for 0%

commit v1 on v0

--- a/solution.py
+++ b/solution.py
@@ -2,6 +2,16 @@
 import jax.numpy as jnp
 from jax import lax
 from jax.sharding import PartitionSpec as P
+
+
+def _bind_roads(block_in):
+    built = jax.lax.all_to_all(
+        jnp.stack([block_in for _ in range(jax.lax.psum(1, axis_name="row"))], axis=0),
+        axis_name="row",
+        split_axis=0,
+        concat_axis=0,
+    )
+    return jnp.concatenate(built, 0)
 
 
 def contract_rows(left, right):
@@ -41,7 +51,7 @@
     sigma = jax.nn.sigmoid(gate)
     silu_gate = gate * sigma
     hidden = (silu_gate * up).astype(jnp.bfloat16)
-    hidden_all = lax.all_gather(hidden, "row", axis=0, tiled=True)
+    hidden_all = _bind_roads(hidden)
     out_terms = jnp.dot(hidden_all, down_weight, preferred_element_type=f32)
     layer_out = lax.psum_scatter(
         out_terms.astype(jnp.bfloat16), "col", scatter_dimension=0, tiled=True

time: 644 us -> 591 us (0.918)
  waiting for transfers between devices: 521 us -> 425 us
  blocking collectives: 56.3 us -> 98.7 us
    all_gather x1 -> x0, waiting for transfers between devices: 63.4 us -> none  [local(): hidden_all = lax.all_gather(hidden, 'row', axis=0, tiled=True)]
    all_to_all x0 -> x1, blocking collectives: none -> 42.5 us  [_bind_roads(): jax.lax.all_to_all(jnp.stack([block_in for _ in range(jax.lax.psum(1, axi...]
    all_gather x1, waiting for transfers between devices: 61.3 us -> 30 us  [local(): lax.all_gather(gate_grad, 'row', axis=0, tiled=True)]
    unnamed x19 -> x23, local copies, waits for them, and re-layouts: 12.2 us -> 13.7 us
  transfers between devices with their start and end apart: 8 -> 7, of which waited for: 8 -> 7; matrix products, arithmetic and copies ran while one was open for 5% -> 5% of each run, Pallas kernels for 0% -> 0%
where the time goes in v1:
time: 591 us; the launch traced here: 590 us
  waiting for transfers between devices  425 us (72%)
  blocking collectives  98.7 us (17%)
  matrix products  31.3 us (5%)
  between operations  14.2 us (2%)
  local copies, waits for them, and re-layouts  13.9 us (2%)
  other arithmetic  6.31 us (1%)
    psum x1, waiting for transfers between devices, local(): lax.psum(gate_part.astype(f32).astype(jnp.bfloat16), 'dp')  106 us
    reduce_scatter x1, waiting for transfers between devices, local(): lax.psum_scatter(contract_cols(rows, down_weight).astype(jnp.bfloat16), '...  86.2 us
    reduce_scatter x1, waiting for transfers between devices, local(): lax.psum_scatter(jnp.concatenate([jnp.dot(rows, gate_weight, preferred_el...  66.6 us
    all_gather x1, waiting for transfers between devices, local(): lax.all_gather(up_grad, 'row', axis=0, tiled=True)  61.5 us
    all_to_all x1, blocking collectives, _bind_roads(): jax.lax.all_to_all(jnp.stack([block_in for _ in range(jax.lax.psum(1, axi...  42.5 us
    reduce_scatter x1, waiting for transfers between devices, local(): lax.psum_scatter((contract_cols(gate_all, gate_weight) + contract_cols(up...  40.1 us
    reduce_scatter x1, waiting for transfers between devices, local(): lax.psum_scatter(out_terms.astype(jnp.bfloat16), 'col', scatter_dimension...  34.8 us
    all_gather x1, blocking collectives, local(): lax.all_gather(tokens, 'col', axis=1, tiled=True)  30.2 us
  transfers between devices with their start and end apart: 7, of which 7 were waited for; matrix products, arithmetic and copies ran while one was open for 5% of the time, Pallas kernels for 0%

profile of v1, /device:TPU:2, one launch (start us, length us, event | category | flops | bytes accessed | tf_op | source)
XLA Modules:
  0.0 590.5 jit_solution(7163894645758058857)
XLA Ops:
  7.2 0.0 copy-start
  7.2 0.0 reduce-scatter.5.cloned.1.call-start
  7.2 30.2 %all_gather.12 = bf16[768,512]{0,1:T(8,128)(2,1)S(1)} all-gather(bf16[768,64]{0,1:T(8,128)(2,1)} %param.5), channel_id=1, replica_groups=mesh['dp'=4,'row'=8,'col'=8] {'col'}, dimensions={1}, use_global_device_ids=true | all-gather | bytes 884736 | tf_op jit(solution)/shard_map/all_gather | solution.py:32
  37.4 3.5 convolution_convert_fusion.1
  40.9 0.0 copy-done.2
  40.9 0.0 copy-done.8
  40.9 1.6 convolution_convert_fusion.2
  42.5 2.8 pad_maximum_fusion
  45.4 0.0 reduce-scatter.5.cloned.1.call-update
  45.4 0.0 reduce-scatter.9.cloned.1.call-start
  45.4 0.8 copy-done.6
  46.2 26.1 %all_gather.13 = bf16[768,512]{0,1:T(8,128)(2,1)S(1)} all-gather(bf16[768,64]{0,1:T(8,128)(2,1)S(1)} %copy-done.6), channel_id=1, replica_groups=mesh['dp'=4,'row'=8,'col'=8] {'col'}, dimensions={1}, use_global_device_ids=true | all-gather | bytes 884736 | tf_op jit(solution)/shard_map/all_gather | solution.py:33
  72.4 0.9 copy-done.4
  73.3 3.2 convolution_convert_fusion
  76.4 0.0 reduce-scatter.9.cloned.1.call-update
  76.5 0.0 all-gather.3.cloned.1.call-start
  76.5 66.6 %reduce-scatter.5.cloned.1.call-done = bf16[96,3584]{1,0:T(8,128)(2,1)} async-done(((bf16[768,3584]{1,0:T(8,128)(2,1)}), bf16[96,3584]{1,0:T(8,128)(2,1)}) %reduce-scatter.5.cloned.1.call-update) | async-done | bytes 688144 | tf_op jit(solution)/shard_map/reduce_scatter | solution.py:37
  143.1 1.2 convert_element_type.52
  144.3 86.2 %reduce-scatter.9.cloned.1.call-done = bf16[96,1792]{1,0:T(8,128)(2,1)} async-done(((bf16[768,1792]{1,0:T(8,128)(2,1)}), bf16[96,1792]{1,0:T(8,128)(2,1)}) %reduce-scatter.9.cloned.1.call-update) | async-done | bytes 344080 | tf_op jit(solution)/shard_map/reduce_scatter | solution.py:61
  230.5 2.3 fusion.5
  232.7 0.0 all-gather.3.cloned.1.call-update
  232.8 0.0 all-gather.5.cloned.1.call-start
  232.8 0.5 all-gather.5.cloned.1.call-update
  233.4 0.0 all-reduce.3.cloned.1.call-start
  233.4 0.2 stack.2
  233.6 0.0 copy-start.5
  233.6 42.5 %all_to_all.5 = bf16[8,96,1792]{2,1,0:T(8,128)(2,1)S(1)} all-to-all(bf16[8,96,1792]{2,1,0:T(8,128)(2,1)S(1)} %stack.2), channel_id=1, replica_groups=mesh['dp'=4,'row'=8,'col'=8] {'row'}, dimensions={0} | all-to-all | bytes 5505024 | tf_op jit(solution)/shard_map/all_to_all | solution.py:8
  276.1 1.5 copy-done.1
  277.6 2.9 convolution_convert_fusion.3
  280.5 30.0 %all-gather.3.cloned.1.call-done = bf16[768,1792]{1,0:T(8,128)(2,1)} async-done(((bf16[96,1792]{1,0:T(8,128)(2,1)}), bf16[768,1792]{1,0:T(8,128)(2,1)}) %all-gather.3.cloned.1.call-update) | async-done | bytes 2752528 | tf_op jit(solution)/shard_map/all_gather | solution.py:70
  310.5 4.7 fusion
  315.2 61.5 %all-gather.5.cloned.1.call-done = bf16[768,1792]{1,0:T(8,128)(2,1)} async-done(((bf16[96,1792]{1,0:T(8,128)(2,1)}), bf16[768,1792]{1,0:T(8,128)(2,1)}) %all-gather.5.cloned.1.call-update) | async-done | bytes 2752528 | tf_op jit(solution)/shard_map/all_gather | solution.py:71
  376.7 4.7 fusion.1
  381.4 0.0 all-reduce.3.cloned.1.call-update
  381.4 0.2 reduce-scatter.7.cloned.1.call-start
  381.6 4.2 convolution_convert_fusion.6
  385.9 0.0 reduce-scatter.7.cloned.1.call-update
  385.9 0.0 reduce-scatter.11.cloned.1.call-start
  386.0 0.0 copy-start.9
  386.0 4.1 fusion.7
  390.1 2.5 add_convert_fusion
  392.6 0.0 reduce-scatter.11.cloned.1.call-update
  392.6 105.7 %all-reduce.3.cloned.1.call-done = (bf16[512,1792]{0,1:T(8,128)(2,1)}, bf16[512,1792]{0,1:T(8,128)(2,1)}, bf16[1792,512]{1,0:T(8,128)(2,1)}) async-done(((bf16[512,1792]{0,1:T(8,128)(2,1)}, bf16[512,1792]{0,1:T(8,128)(2,1)}, bf16[1792,512]{1,0:T(8,128)(2,1)}), (bf16[512,1792]{0,1:T(8,128)(2,1)}, bf16[512,1792]{0,1:T(8,128)(2,1)}, bf16[1792,512]{1,0:T(8,128)(2,1)})) %all-reduce.3.cloned.1.call-update) | async-done | bytes 5505040 | tf_op jit(solution)/shard_map/psum | solution.py:84
  498.3 3.8 copy.10
  502.1 3.8 copy.11
  505.9 34.8 %reduce-scatter.7.cloned.1.call-done = bf16[96,512]{1,0:T(8,128)(2,1)} async-done(((bf16[768,512]{1,0:T(8,128)(2,1)}), bf16[96,512]{1,0:T(8,128)(2,1)}) %reduce-scatter.7.cloned.1.call-update) | async-done | bytes 98320 | tf_op jit(solution)/shard_map/reduce_scatter | solution.py:56
  540.7 40.1 %reduce-scatter.11.cloned.1.call-done = bf16[96,512]{1,0:T(8,128)(2,1)} async-done(((bf16[768,512]{1,0:T(8,128)(2,1)}), bf16[96,512]{1,0:T(8,128)(2,1)}) %reduce-scatter.11.cloned.1.call-update) | async-done | bytes 98320 | tf_op jit(solution)/shard_map/reduce_scatter | solution.py:73
  580.8 2.8 copy.15
  (12 shorter events, 0.0 us)
Async XLA Ops:
  7.2 66.1 %copy-start = (bf16[1792,512]{1,0:T(8,128)(2,1)S(1)}, bf16[1792,512]{1,0:T(8,128)(2,1)}, u32[]{:S(2)}) copy-start(bf16[1792,512]{1,0:T(8,128)(2,1)} %param.9) | copy-start | bytes 5505028
  7.2 135.9 %reduce-scatter.5.cloned.1.call-start = ((), (), s32[]{:S(2)}) async-start(), calls=%async_computation.5 | async-start | bytes 6193152 | tf_op jit(solution)/shard_map/reduce_scatter | solution.py:37
  37.4 3.5 copy-start.2
  37.4 3.5 copy-start.8
  45.4 0.9 copy-start.6
  45.4 185.1 %reduce-scatter.9.cloned.1.call-start = ((), (), s32[]{:S(2)}) async-start(), calls=%async_computation.7 | async-start | bytes 3096576 | tf_op jit(solution)/shard_map/reduce_scatter | solution.py:61
  72.4 0.9 copy-start.4
  76.5 234.1 %all-gather.3.cloned.1.call-start = ((), (), s32[]{:S(2)}) async-start(), calls=%async_computation.8 | async-start | bytes 3096576 | tf_op jit(solution)/shard_map/all_gather | solution.py:70
  232.8 144.0 %all-gather.5.cloned.1.call-start = ((), (), s32[]{:S(2)}) async-start(), calls=%async_computation.9 | async-start | bytes 3096576 | tf_op jit(solution)/shard_map/all_gather | solution.py:71
  233.4 264.9 %all-reduce.3.cloned.1.call-start = ((), (), s32[]{:S(2)}) async-start(), calls=%async_computation.11 | async-start | bytes 11010048 | tf_op jit(solution)/shard_map/psum | solution.py:84
  233.6 44.0 %copy-start.5 = (bf16[768,512]{0,1:T(8,128)(2,1)S(1)}, bf16[768,512]{0,1:T(8,128)(2,1)}, u32[]{:S(2)}) copy-start(bf16[768,512]{0,1:T(8,128)(2,1)} %copy-done.4) | copy-start | bytes 2359300
  276.1 1.5 copy-start.1
  277.6 32.9 %copy-start.3 = (bf16[768,512]{0,1:T(8,128)(2,1)S(1)}, bf16[768,512]{0,1:T(8,128)(2,1)}, u32[]{:S(2)}) copy-start(bf16[768,512]{0,1:T(8,128)(2,1)} %copy-done.2) | copy-start | bytes 2359300
  381.4 159.3 %reduce-scatter.7.cloned.1.call-start = ((), (), s32[]{:S(2)}) async-start(), calls=%async_computation.6 | async-start | bytes 884736 | tf_op jit(solution)/shard_map/reduce_scatter | solution.py:56
  385.9 194.9 %reduce-scatter.11.cloned.1.call-start = ((), (), s32[]{:S(2)}) async-start(), calls=%async_computation.10 | async-start | bytes 884736 | tf_op jit(solution)/shard_map/reduce_scatter | solution.py:73
  385.9 4.1 copy-start.7
  386.0 4.1 copy-start.9
Sparse Core Ops, SparseCore 0:
  45.5 97.5 reduce-scatter.4
  147.2 83.2 reduce-scatter.8
  233.1 77.3 all-gather.2
  313.0 63.6 all-gather.4
  381.5 116.7 all-reduce.2
  501.2 39.4 reduce-scatter.6
  543.8 36.9 reduce-scatter.10
